TPU v7x, 32 devices: a whole 2x2x4 slice. The times are simulated.
32 devices in a mesh: section: 4 (over z), dp: 2 (over core), seq: 4 (over y, x).
Axes of the slice: x: 2, y: 2, z: 4, core: 2. Of those that a mesh axis runs over, the one named last changes fastest.
Arguments:
- qkv: bfloat16 [4, 4, 256, 6144], P('section', 'dp', 'seq'), may hold values from -5 to 5
- stream_lengths: int32 [4, 4], P('section'), may hold values from 1 to 192, 256 in all within a row
- doc_lengths: int32 [4, 4, 8], P('section'), may hold values from 1 to 128, 256 in all within a row
- hand_over: int32 [4, 2], P('section'), may hold values from 0 to 1
Outputs:
- handoff: bfloat16 [4, 4, 256, 4096], P('section', 'dp', 'seq')
Inputs may be any that keep to these rules, and one draw needn't show every extreme that they name: `stream_lengths`: each entry is the length of one row; the 4 entries of one section, taken together, sum to 256, and in each section one entry is exactly the most.
All inputs are finite; a program needn't handle non-finite values.
Results may differ from a plain program's by a relative error of at most 0.0013.
Values may be sent and summed in bfloat16 or wider, within the bound.
No kernel may reach another device: no remote copies, remote signals or barrier semaphores. Data moves between devices by JAX's collectives and lax.ppermute only.
A program may use at most 64 MiB of HBM per device.

v0:
```python
import jax
import jax.numpy as jnp
from jax import lax
from jax.sharding import PartitionSpec as P

H = 32
HD = 128
KV_HEADS = 8
D = 4096
RPR = 2


def swapped(block, axis, distance):
    count = lax.axis_size(axis)
    route = []
    for low in range(count):
        high = low | 1 << distance
        if high != low and high < count:
            route += [(low, high), (high, low)]
    return lax.ppermute(block, axis, route)


def passed_along(value, axis, steps):
    count = lax.axis_size(axis)
    pairs = [(source, (source + steps) % count) for source in range(count)]
    return lax.ppermute(value, axis, pairs)


def attend(row_data, row_ids, stream_lengths, doc_ends, seq_count):
    seg_len = row_data.shape[1]
    length = seg_len * seq_count
    heads_dev = H // seq_count
    group_size = H // KV_HEADS
    kv_dev = max(1, heads_dev // group_size)
    copies = max(1, group_size // heads_dev)
    group_local = heads_dev // kv_dev
    q_width = H * HD
    key_value_width = KV_HEADS * HD
    query_send = row_data[..., :q_width].reshape(RPR, seg_len, seq_count, heads_dev * HD)
    key_portion = row_data[..., q_width : q_width + key_value_width]
    value_part = row_data[..., q_width + key_value_width :]
    key_send = jnp.repeat(key_portion.reshape(RPR, seg_len, KV_HEADS, HD), copies, axis=2).reshape(
        RPR, seg_len, seq_count, kv_dev * HD
    )
    value_send = jnp.repeat(value_part.reshape(RPR, seg_len, KV_HEADS, HD), copies, axis=2).reshape(
        RPR, seg_len, seq_count, kv_dev * HD
    )
    query_heads, kv_heads = (
        lax.all_to_all(query_send, "seq", split_axis=2, concat_axis=1, tiled=True),
        lax.all_to_all(
            jnp.concatenate([key_send, value_send], axis=3),
            "seq",
            split_axis=2,
            concat_axis=1,
            tiled=True,
        ),
    )
    key_block = kv_heads[:, :, 0, : kv_dev * HD]
    value_block = kv_heads[:, :, 0, kv_dev * HD :]
    query_tile_rows = query_heads[:, :, 0, :]
    positions = jnp.arange(length, dtype=jnp.int32)
    row_match = (
        jnp.arange(doc_ends.shape[0], dtype=jnp.int32)[None, :] == row_ids[:, None]
    ).astype(jnp.int32)
    ends_rows = jnp.sum(row_match[:, :, None] * doc_ends[None, :, :], axis=1)
    lengths_rows = jnp.sum(row_match * stream_lengths[None, :], axis=1)
    doc_index = jnp.sum(
        (positions[None, :, None] >= ends_rows[:, None, :]).astype(jnp.int32), axis=2
    )
    causal = positions[:, None] >= positions[None, :]
    score_scale = HD ** (-0.5)
    results = []
    for slot_index in range(RPR):
        allowed = causal & (doc_index[slot_index][:, None] == doc_index[slot_index][None, :])
        query_row = query_tile_rows[slot_index].reshape(length, kv_dev, group_local, HD)
        key_row = key_block[slot_index].reshape(length, kv_dev, HD)
        value_row = value_block[slot_index].reshape(length, kv_dev, HD)
        scores = (
            jnp.einsum("qkgd,skd->kgqs", query_row, key_row, preferred_element_type=jnp.float32)
            * score_scale
        )
        row_top = jnp.max(jnp.where(allowed, scores, -jnp.inf), axis=-1, keepdims=True)
        weights = jnp.where(allowed, jnp.exp(scores - row_top), 0.0)
        row_total = jnp.sum(weights, axis=-1)
        rounded = weights.astype(jnp.bfloat16)
        summed = jnp.einsum(
            "kgqs,skd->qkgd", rounded, value_row, preferred_element_type=jnp.float32
        )
        result = summed / jnp.transpose(row_total, (2, 0, 1))[..., None]
        valid = (positions < lengths_rows[slot_index]).astype(jnp.float32)
        result = result * valid[:, None, None, None]
        results.append(result.reshape(length, heads_dev * HD).astype(jnp.bfloat16))
    return jnp.stack(results, axis=0)


def shards(qkv, stream_lengths, doc_lengths, hand_over):
    seq_count = lax.axis_size("seq")
    replica = lax.axis_index("dp")
    partner = jnp.bitwise_xor(replica, 1)
    handed = lax.dynamic_index_in_dim(hand_over[0], replica, 0, keepdims=False)
    partner_handed = lax.dynamic_index_in_dim(hand_over[0], partner, 0, keepdims=False)
    own_rows = qkv[0]
    seg_len = own_rows.shape[1]
    doc_ends = jnp.cumsum(doc_lengths[0], axis=1)
    lengths_all = stream_lengths[0]
    given = lax.dynamic_index_in_dim(own_rows, handed, 0, keepdims=True)
    kept = lax.dynamic_index_in_dim(own_rows, 1 - handed, 0, keepdims=True)
    received = swapped(given, "dp", 0)
    row_ids = jnp.stack([2 * replica + 1 - handed, 2 * partner + partner_handed])
    attention_output = attend(
        jnp.concatenate([kept, received], axis=0), row_ids, lengths_all, doc_ends, seq_count
    )
    grouped = attention_output.reshape(RPR, seq_count, seg_len, attention_output.shape[2])
    tokens = lax.all_to_all(grouped, "seq", split_axis=1, concat_axis=3, tiled=True)
    tokens = passed_along(tokens, "section", 1)
    return tokens.reshape(1, RPR, seg_len, D)


def solution(mesh):
    return jax.shard_map(
        shards,
        mesh=mesh,
        in_specs=(
            P("section", "dp", "seq", None),
            P("section", None),
            P("section", None, None),
            P("section", None),
        ),
        out_specs=P("section", "dp", "seq", None),
        check_vma=False,
    )
```

profile of v0, /device:TPU:0, one launch (start us, length us, event | category | flops | bytes accessed | tf_op | source)
XLA Modules:
  0.0 89.6 jit_solution(12574448168181887721)
XLA Ops:
  0.0 0.0 copy-start
  0.0 0.0 copy-start.1
  0.0 1.4 %constant_dynamic-slice_fusion = (s32[1,1]{1,0:T(1,128)}, s32[1,1]{1,0:T(1,128)}) fusion(s32[1,2]{1,0:T(1,128)} %param.7, s32[]{:T(128)S(6)} %select_n.30, s32[]{:T(128)S(6)} %select_n.27), kind=kLoop, calls=%fused_computation.53 | loop fusion | bytes 24 | tf_op jit(solution)/shard_map/jit(dynamic_index_in_dim)/dynamic_slice | solution.py:101
  4.9 1.5 %dynamic-slice_bitcast_fusion.1 = (bf16[1,64,6144]{2,1,0:T(8,128)(2,1)S(1)}, bf16[1,64,6144]{2,1,0:T(8,128)(2,1)S(1)}) fusion(bf16[1,2,64,6144]{3,2,1,0:T(8,128)(2,1)} %param.4, s32[]{:T(128)S(6)} %select_n.28, s32[]{:T(128)S(6)} %select_n.29), kind=kLoop, calls=%fused_computation.34 | loop fusion | bytes 3145736 | tf_op jit(solution)/shard_map/jit(dynamic_index_in_dim)/dynamic_slice | solution.py:107
  6.3 0.6 collective-permute-start
  7.6 0.0 copy-done
  7.6 0.2 reduce_window_sum.14
  8.4 0.1 pad_add_fusion
  8.5 0.0 copy-done.1
  8.5 0.2 select_reduce_fusion
  8.7 0.7 fusion.38
  9.4 0.6 compare_convert_fusion.1
  10.0 0.1 fusion.30
  10.1 0.1 multiply_reduce_fusion
  10.2 0.1 convert_reduce_fusion
  10.3 0.0 collective-permute-done
  10.3 0.2 reshape_reshape_broadcast_in_dim_reshape.6
  10.5 0.2 reshape_reshape_broadcast_in_dim_reshape.7
  10.7 0.2 pad_maximum_fusion.2
  10.9 0.9 copy.54
  11.8 4.7 %all-to-all-start = ((bf16[2,64,4,512]{3,1,0,2:T(8,128)(2,1)}), bf16[2,64,4,512]{3,1,0,2:T(8,128)(2,1)S(1)}, u32[]{:S(2)}, u32[]{:S(2)}) async-start(bf16[2,64,4,512]{3,1,0,2:T(8,128)(2,1)} %copy.54), calls=%async_computation | async-start | bytes 1048576 | tf_op jit(solution)/shard_map/all_to_all | solution.py:50
  16.5 0.1 pad_maximum_fusion
  16.6 1.1 %copy.88 = bf16[2,8,4,8,1024]{4,3,1,0,2:T(8,128)(2,1)} copy(bf16[2,8,4,8,1024]{4,3,2,1,0:T(8,128)(2,1)S(1)} %bitcast.113) | data formatting | bytes 2097152 | tf_op jit(solution)/shard_map/reshape | solution.py:39
  17.7 7.5 %all-to-all-done = bf16[2,64,4,512]{3,1,0,2:T(8,128)(2,1)S(1)} async-done(((bf16[2,64,4,512]{3,1,0,2:T(8,128)(2,1)}), bf16[2,64,4,512]{3,1,0,2:T(8,128)(2,1)S(1)}, u32[]{:S(2)}, u32[]{:S(2)}) %all-to-all-start) | async-done | bytes 524320 | tf_op jit(solution)/shard_map/all_to_all | solution.py:50
  25.2 3.5 %all-to-all-start.1 = ((bf16[2,64,4,1024]{3,1,0,2:T(8,128)(2,1)}), bf16[2,64,4,1024]{3,1,0,2:T(8,128)(2,1)S(1)}, u32[]{:S(2)}, u32[]{:S(2)}) async-start(bf16[2,64,4,1024]{3,1,0,2:T(8,128)(2,1)} %bitcast.111), calls=%async_computation.1 | async-start | bytes 2097152 | tf_op jit(solution)/shard_map/all_to_all | solution.py:49
  28.7 0.7 compare_convert_fusion
  29.4 0.1 fusion.29
  29.6 0.1 fusion.28
  29.8 0.1 copy.57
  29.9 0.1 copy.56
  30.0 0.1 copy.64
  30.1 0.1 copy.63
  30.2 12.0 %all-to-all-done.1 = bf16[2,64,4,1024]{3,1,0,2:T(8,128)(2,1)S(1)} async-done(((bf16[2,64,4,1024]{3,1,0,2:T(8,128)(2,1)}), bf16[2,64,4,1024]{3,1,0,2:T(8,128)(2,1)S(1)}, u32[]{:S(2)}, u32[]{:S(2)}) %all-to-all-start.1) | async-done | bytes 1048608 | tf_op jit(solution)/shard_map/all_to_all | solution.py:49
  42.1 0.1 fusion.35
  42.2 0.4 reshape_squeeze.20
  42.6 0.5 fusion.26
  43.1 0.9 fusion.40
  44.0 0.3 fusion.14
  44.3 0.3 copy.62
  44.6 0.4 convert_element_type.63
  45.0 0.4 reshape_squeeze.23
  45.4 0.5 fusion.24
  45.8 0.9 fusion.39
  46.7 0.3 fusion.15
  47.1 0.3 copy.68
  47.4 0.4 convert_element_type.67
  47.8 0.1 pad_maximum_fusion.1
  47.9 0.1 copy.69
  47.9 16.1 %all_to_all.51 = bf16[2,4,64,1024]{3,2,0,1:T(8,128)(2,1)S(1)} all-to-all(bf16[2,4,64,1024]{3,2,0,1:T(8,128)(2,1)S(1)} %copy.69), channel_id=1, replica_groups=mesh['section'=4,'dp'=2,'seq'=4] {'seq'}, dimensions={1} | all-to-all | bytes 2097152 | tf_op jit(solution)/shard_map/all_to_all | solution.py:114
  64.0 0.1 copy.82
  64.1 1.6 %collective-permute-start.1 = (bf16[2,1,64,4096]{3,2,0,1:T(8,128)(2,1)S(1)}, bf16[2,1,64,4096]{3,2,0,1:T(8,128)(2,1)S(1)}, u32[]{:S(2)}, u32[]{:S(2)}) collective-permute-start(bf16[2,1,64,4096]{3,2,0,1:T(8,128)(2,1)S(1)} %bitcast.116), channel_id=1, source_target_pairs={{0,8},{8,16},{16,24},{24,0},{1,9},{9,17},{17,25},{25,1},{2,10},{10... | collective-permute-start | bytes 3145736 | tf_op jit(solution)/shard_map/ppermute | solution.py:26
  65.7 22.9 %collective-permute-done.1 = bf16[2,1,64,4096]{3,2,0,1:T(8,128)(2,1)S(1)} collective-permute-done((bf16[2,1,64,4096]{3,2,0,1:T(8,128)(2,1)S(1)}, bf16[2,1,64,4096]{3,2,0,1:T(8,128)(2,1)S(1)}, u32[]{:S(2)}, u32[]{:S(2)}) %collective-permute-start.1) | collective-permute-done | bytes 1048608 | tf_op jit(solution)/shard_map/ppermute | solution.py:26
  88.7 1.0 %copy.90 = bf16[1,2,64,4096]{3,2,1,0:T(8,128)(2,1)} copy(bf16[1,2,64,4096]{3,2,1,0:T(8,128)(2,1)S(1)} %bitcast.117) | data formatting | bytes 2097152
  (4 shorter events, 0.1 us)
Async XLA Ops:
  0.0 7.6 %copy-start = (s32[1,4,8]{2,1,0:T(4,128)S(1)}, s32[1,4,8]{2,1,0:T(4,128)}, u32[]{:S(2)}) copy-start(s32[1,4,8]{2,1,0:T(4,128)} %param.6) | copy-start | bytes 388
  0.0 8.5 %copy-start.1 = (s32[1,4]{1,0:T(1,128)S(1)}, s32[1,4]{1,0:T(1,128)}, u32[]{:S(2)}) copy-start(s32[1,4]{1,0:T(1,128)} %param.5) | copy-start | bytes 52
  6.3 3.9 %collective-permute-start = (bf16[1,64,6144]{2,1,0:T(8,128)(2,1)S(1)}, bf16[1,64,6144]{2,1,0:T(8,128)(2,1)S(1)}, u32[]{:S(2)}, u32[]{:S(2)}) collective-permute-start(bf16[1,64,6144]{2,1,0:T(8,128)(2,1)S(1)} %get-tuple-element.8), channel_id=1, source_target_pairs={{0,4},{4,0},{1,5},{5,1},{2,6},{6,2},{3,7},{7,3},{8,12},{12,8},{9,1... | collective-permute-start | bytes 2359304 | tf_op jit(solution)/shard_map/ppermute | solution.py:20
  11.8 13.4 %all-to-all-start = ((bf16[2,64,4,512]{3,1,0,2:T(8,128)(2,1)}), bf16[2,64,4,512]{3,1,0,2:T(8,128)(2,1)S(1)}, u32[]{:S(2)}, u32[]{:S(2)}) async-start(bf16[2,64,4,512]{3,1,0,2:T(8,128)(2,1)} %copy.54), calls=%async_computation | async-start | bytes 1048576 | tf_op jit(solution)/shard_map/all_to_all | solution.py:50
  25.2 16.9 %all-to-all-start.1 = ((bf16[2,64,4,1024]{3,1,0,2:T(8,128)(2,1)}), bf16[2,64,4,1024]{3,1,0,2:T(8,128)(2,1)S(1)}, u32[]{:S(2)}, u32[]{:S(2)}) async-start(bf16[2,64,4,1024]{3,1,0,2:T(8,128)(2,1)} %bitcast.111), calls=%async_computation.1 | async-start | bytes 2097152 | tf_op jit(solution)/shard_map/all_to_all | solution.py:49
  64.1 24.6 %collective-permute-start.1 = (bf16[2,1,64,4096]{3,2,0,1:T(8,128)(2,1)S(1)}, bf16[2,1,64,4096]{3,2,0,1:T(8,128)(2,1)S(1)}, u32[]{:S(2)}, u32[]{:S(2)}) collective-permute-start(bf16[2,1,64,4096]{3,2,0,1:T(8,128)(2,1)S(1)} %bitcast.116), channel_id=1, source_target_pairs={{0,8},{8,16},{16,24},{24,0},{1,9},{9,17},{17,25},{25,1},{2,10},{10... | collective-permute-start | bytes 3145736 | tf_op jit(solution)/shard_map/ppermute | solution.py:26
where the time goes:
time: 90 us; the launch traced here: 89.6 us
  waiting for transfers between devices  42.4 us (47%)
  blocking collectives  16.1 us (18%)
  starting transfers between devices  10.4 us (12%)
  local copies, waits for them, and re-layouts  9.62 us (11%)
  between operations  5.03 us (6%)
  other arithmetic  4.47 us (5%)
  matrix products  1.61 us (2%)
    ppermute x1, waiting for transfers between devices, passed_along(): return lax.ppermute(value, axis, pairs)  22.9 us
    all_to_all x1, blocking collectives, shards(): lax.all_to_all(grouped, 'seq', split_axis=1, concat_axis=3, tiled=True)  16.1 us
    all_to_all x1, waiting for transfers between devices, attend(): lax.all_to_all(query_send, 'seq', split_axis=2, concat_axis=1, tiled=True)  12 us
    all_to_all x1, waiting for transfers between devices, attend(): lax.all_to_all(jnp.concatenate([key_send, value_send], axis=3), 'seq', sp...  7.52 us
    all_to_all x1, starting transfers between devices, attend(): lax.all_to_all(jnp.concatenate([key_send, value_send], axis=3), 'seq', sp...  4.71 us
    all_to_all x1, starting transfers between devices, attend(): lax.all_to_all(query_send, 'seq', split_axis=2, concat_axis=1, tiled=True)  3.52 us
  transfers between devices with their start and end apart: 4, of which 3 were waited for; matrix products, arithmetic and copies ran while one was open for 5% of the time, Pallas kernels for 0%

commit v1 on v0

--- a/solution.py
+++ b/solution.py
@@ -1,3 +1,4 @@
+import functools
 import jax
 import jax.numpy as jnp
 from jax import lax
@@ -8,6 +9,31 @@
 KV_HEADS = 8
 D = 4096
 RPR = 2
+
+
+def patch_follow(xx, along_axis):
+    item_now, base_arr = (lax.axis_size(along_axis), lax.axis_index(along_axis))
+    block_next = xx.shape[2] // item_now
+    z = list(xx.shape)
+    z[2] = block_next
+    block_now = z[1]
+    z[1] = block_now * item_now
+    moved = jnp.zeros(z, xx.dtype)
+    idx = 0
+    while idx < item_now:
+        wide_out = lax.dynamic_slice_in_dim(xx, (base_arr ^ idx) * block_next, block_next, axis=2)
+        if idx:
+            wide_out = lax.ppermute(
+                wide_out, along_axis, tuple(((t, t ^ idx) for t in range(item_now)))
+            )
+        moved = lax.dynamic_update_slice_in_dim(
+            moved, wide_out, (base_arr ^ idx) * block_now, axis=1
+        )
+        idx += 1
+    return moved
+
+
+fix_the_ports = functools.partial(patch_follow, along_axis="seq")
 
 
 def swapped(block, axis, distance):
@@ -46,7 +72,7 @@
         RPR, seg_len, seq_count, kv_dev * HD
     )
     query_heads, kv_heads = (
-        lax.all_to_all(query_send, "seq", split_axis=2, concat_axis=1, tiled=True),
+        fix_the_ports(query_send),
         lax.all_to_all(
             jnp.concatenate([key_send, value_send], axis=3),
             "seq",

time: 90 us -> 105 us (1.17)
  local copies, waits for them, and re-layouts: 9.62 us -> 28.9 us
  waiting for transfers between devices: 42.4 us -> 34.7 us
  matrix products: 1.61 us -> 7.05 us
  other arithmetic: 4.47 us -> 2.52 us
    ppermute x0 -> x3, waiting for transfers between devices: none -> 12.5 us  [patch_follow(): lax.ppermute(wide_out, along_axis, tuple(((t, t ^ idx) for t in range(ite...]
    dynamic_update_slice x0 -> x4, local copies, waits for them, and re-layouts: none -> 12.4 us  [patch_follow(): lax.dynamic_update_slice_in_dim(moved, wide_out, (base_arr ^ idx) * block...]
    all_to_all x1 -> x0, waiting for transfers between devices: 12 us -> none  [attend(): lax.all_to_all(query_send, 'seq', split_axis=2, concat_axis=1, tiled=True)]
    all_to_all x1, waiting for transfers between devices: 7.52 us -> 0.01 us  [attend(): lax.all_to_all(jnp.concatenate([key_send, value_send], axis=3), 'seq', sp...]
    squeeze x0 -> x5, local copies, waits for them, and re-layouts: none -> 4.82 us  [attend(): query_tile_rows = query_heads[:, :, 0, :]]
    ppermute x0 -> x3, starting transfers between devices: none -> 4.04 us  [patch_follow(): lax.ppermute(wide_out, along_axis, tuple(((t, t ^ idx) for t in range(ite...]
    sub x0 -> x2, matrix products: none -> 3.97 us  [attend(): weights = jnp.where(allowed, jnp.exp(scores - row_top), 0.0)]
    all_to_all x1 -> x0, starting transfers between devices: 3.52 us -> none  [attend(): lax.all_to_all(query_send, 'seq', split_axis=2, concat_axis=1, tiled=True)]
  transfers between devices with their start and end apart: 4 -> 6, of which waited for: 3 -> 3; matrix products, arithmetic and copies ran while one was open for 5% -> 20% of each run, Pallas kernels for 0% -> 0%
where the time goes in v1:
time: 105 us
  waiting for transfers between devices  34.7 us (33%)
  local copies, waits for them, and re-layouts  28.9 us (28%)
  blocking collectives  16.2 us (15%)
  starting transfers between devices  10.3 us (10%)
  matrix products  7.05 us (7%)
  between operations  5.15 us (5%)
  other arithmetic  2.52 us (2%)
    ppermute x1, waiting for transfers between devices, passed_along(): return lax.ppermute(value, axis, pairs)  22.3 us
    all_to_all x1, blocking collectives, shards(): lax.all_to_all(grouped, 'seq', split_axis=1, concat_axis=3, tiled=True)  16.2 us
    ppermute x3, waiting for transfers between devices, patch_follow(): lax.ppermute(wide_out, along_axis, tuple(((t, t ^ idx) for t in range(ite...  12.5 us
    dynamic_update_slice x4, local copies, waits for them, and re-layouts, patch_follow(): lax.dynamic_update_slice_in_dim(moved, wide_out, (base_arr ^ idx) * block...  12.4 us
    squeeze x5, local copies, waits for them, and re-layouts, attend(): query_tile_rows = query_heads[:, :, 0, :]  4.82 us
    all_to_all x1, starting transfers between devices, attend(): lax.all_to_all(jnp.concatenate([key_send, value_send], axis=3), 'seq', sp...  4.19 us
    ppermute x3, starting transfers between devices, patch_follow(): lax.ppermute(wide_out, along_axis, tuple(((t, t ^ idx) for t in range(ite...  4.04 us
    sub x2, matrix products, attend(): weights = jnp.where(allowed, jnp.exp(scores - row_top), 0.0)  3.97 us
  transfers between devices with their start and end apart: 6, of which 3 were waited for; matrix products, arithmetic and copies ran while one was open for 20% of the time, Pallas kernels for 0%

profile of v1, /device:TPU:0, one launch (start us, length us, event | category | flops | bytes accessed | tf_op | source)
XLA Modules:
  0.0 105.0 jit_solution(6270119990654447246)
XLA Ops:
  0.0 1.4 %constant_dynamic-slice_fusion.4 = (s32[1,1]{1,0:T(1,128)}, s32[1,1]{1,0:T(1,128)}) fusion(s32[1,2]{1,0:T(1,128)} %param.7, s32[]{:T(128)S(6)} %select_n.54, s32[]{:T(128)S(6)} %select_n.51), kind=kLoop, calls=%fused_computation.49 | loop fusion | bytes 24 | tf_op jit(solution)/shard_map/jit(dynamic_index_in_dim)/dynamic_slice | solution.py:127
  4.9 0.0 copy-start
  4.9 0.0 copy-start.1
  4.9 1.5 %dynamic-slice_bitcast_fusion.1 = (bf16[1,64,6144]{2,1,0:T(8,128)(2,1)S(1)}, bf16[1,64,6144]{2,1,0:T(8,128)(2,1)S(1)}) fusion(bf16[1,2,64,6144]{3,2,1,0:T(8,128)(2,1)} %param.4, s32[]{:T(128)S(6)} %select_n.52, s32[]{:T(128)S(6)} %select_n.53), kind=kLoop, calls=%fused_computation.33 | loop fusion | bytes 3145736 | tf_op jit(solution)/shard_map/jit(dynamic_index_in_dim)/dynamic_slice | solution.py:133
  6.4 0.6 collective-permute-start
  6.9 0.0 copy-done
  6.9 0.2 reduce_window_sum.14
  8.4 0.1 pad_add_fusion
  8.5 0.1 fusion.30
  8.6 0.1 multiply_reduce_fusion
  8.7 0.1 convert_reduce_fusion
  8.8 0.0 copy-done.1
  8.8 0.2 select_reduce_fusion
  9.0 0.6 fusion.38
  9.6 0.1 fusion.24
  9.7 0.1 fusion.25
  9.8 0.0 collective-permute-done
  9.8 0.2 reshape_reshape_broadcast_in_dim_reshape.7
  10.0 0.2 reshape_reshape_broadcast_in_dim_reshape.6
  10.2 0.1 pad_maximum_fusion
  10.3 0.8 reshape.99
  11.1 3.1 %constant_dynamic-slice_fusion = (bf16[2,64,1,1024]{3,2,1,0:T(2,128)(2,1)}, bf16[2,64,1,1024]{3,2,1,0:T(2,128)(2,1)}, bf16[2,64,1,1024]{3,2,1,0:T(2,128)(2,1)}, bf16[2,64,1,1024]{3,2,1,0:T(2,128)(2,1)S(1)}) fusion(bf16[2,64,4,1024]{3,2,1,0:T(4,128)(2,1)S(1)} %reshape.99, s32[]{:T(128)S(6)} %select_n.61, s32[]{:T(128)S(6)} %select_n.59, s32[]{:T(128)S(6)} %select_n.57, ...), kind=kLoop, calls=%fused_computation.45 | loop fusion | bytes 2097168 | tf_op jit(solution)/shard_map/dynamic_slice | solution.py:24
  14.3 2.5 %collective-permute-start.1 = (bf16[2,64,1,1024]{3,2,1,0:T(2,128)(2,1)}, bf16[2,64,1,1024]{3,2,1,0:T(2,128)(2,1)}, u32[]{:S(2)}, u32[]{:S(2)}) collective-permute-start(bf16[2,64,1,1024]{3,2,1,0:T(2,128)(2,1)} %get-tuple-element.13), channel_id=1, source_target_pairs={{0,1},{1,0},{2,3},{3,2},{4,5},{5,4},{6,7},{7,6},{8,9},{9,8},{10,11... | collective-permute-start | bytes 786440 | tf_op jit(solution)/shard_map/ppermute | solution.py:26
  16.8 1.5 %collective-permute-start.2 = (bf16[2,64,1,1024]{3,2,1,0:T(2,128)(2,1)}, bf16[2,64,1,1024]{3,2,1,0:T(2,128)(2,1)}, u32[]{:S(2)}, u32[]{:S(2)}) collective-permute-start(bf16[2,64,1,1024]{3,2,1,0:T(2,128)(2,1)} %get-tuple-element.12), channel_id=1, source_target_pairs={{0,2},{1,3},{2,0},{3,1},{4,6},{5,7},{6,4},{7,5},{8,10},{9,11},{10,... | collective-permute-start | bytes 786440 | tf_op jit(solution)/shard_map/ppermute | solution.py:26
  18.3 0.0 collective-permute-start.3
  18.3 0.2 pad_maximum_fusion.2
  18.5 0.9 copy.63
  19.4 4.2 %all-to-all-start = ((bf16[2,64,4,512]{3,1,0,2:T(8,128)(2,1)}), bf16[2,64,4,512]{3,1,0,2:T(8,128)(2,1)S(1)}, u32[]{:S(2)}, u32[]{:S(2)}) async-start(bf16[2,64,4,512]{3,1,0,2:T(8,128)(2,1)} %copy.63), calls=%async_computation | async-start | bytes 1048576 | tf_op jit(solution)/shard_map/all_to_all | solution.py:76
  23.6 0.6 compare_convert_fusion
  24.3 0.5 compare_convert_fusion.1
  24.8 0.5 copy.93
  25.4 0.1 squeeze.32
  25.4 2.5 %dynamic_update_slice.16 = bf16[2,256,1024]{1,2,0:T(8,128)(2,1)S(1)} dynamic-update-slice(bf16[2,256,1024]{1,2,0:T(8,128)(2,1)S(1)} %squeeze.32, bf16[2,64,1024]{1,2,0:T(8,128)(2,1)S(1)} %bitcast.111, s32[]{:T(128)} %constant.42.clone.1, s32[]{:T(128)S(6)} %select_n.56, s32[]{:T(128)} %constant.42.clone.1) | dynamic-update-slice | bytes 524292 | tf_op jit(solution)/shard_map/dynamic_update_slice | solution.py:29
  27.9 2.0 %collective-permute-done.1 = bf16[2,64,1,1024]{3,2,1,0:T(2,128)(2,1)} collective-permute-done((bf16[2,64,1,1024]{3,2,1,0:T(2,128)(2,1)}, bf16[2,64,1,1024]{3,2,1,0:T(2,128)(2,1)}, u32[]{:S(2)}, u32[]{:S(2)}) %collective-permute-start.1) | collective-permute-done | bytes 262176 | tf_op jit(solution)/shard_map/ppermute | solution.py:26
  29.9 1.4 %copy.94 = bf16[2,64,1,1024]{1,3,0,2:T(8,128)(2,1)S(1)} copy(bf16[2,64,1,1024]{3,2,1,0:T(2,128)(2,1)} %collective-permute-done.1) | data formatting | bytes 524288 | tf_op jit(solution)/shard_map/squeeze | solution.py:86
  31.3 4.1 %dynamic_update_slice.17 = bf16[2,256,1024]{1,2,0:T(8,128)(2,1)S(1)} dynamic-update-slice(bf16[2,256,1024]{1,2,0:T(8,128)(2,1)S(1)} %dynamic_update_slice.16, bf16[2,64,1024]{1,2,0:T(8,128)(2,1)S(1)} %bitcast.113, s32[]{:T(128)} %constant.42.clone.1, s32[]{:T(128)S(6)} %select_n.58, s32[]{:T(128)} %constant.42.clone.1) | dynamic-update-slice | bytes 524292 | tf_op jit(solution)/shard_map/dynamic_update_slice | solution.py:29
  35.4 10.5 %collective-permute-done.2 = bf16[2,64,1,1024]{3,2,1,0:T(2,128)(2,1)} collective-permute-done((bf16[2,64,1,1024]{3,2,1,0:T(2,128)(2,1)}, bf16[2,64,1,1024]{3,2,1,0:T(2,128)(2,1)}, u32[]{:S(2)}, u32[]{:S(2)}) %collective-permute-start.2) | collective-permute-done | bytes 262176 | tf_op jit(solution)/shard_map/ppermute | solution.py:26
  45.9 1.4 %copy.95 = bf16[2,64,1,1024]{1,3,0,2:T(8,128)(2,1)S(1)} copy(bf16[2,64,1,1024]{3,2,1,0:T(2,128)(2,1)} %collective-permute-done.2) | data formatting | bytes 524288 | tf_op jit(solution)/shard_map/squeeze | solution.py:86
  47.4 2.1 %dynamic_update_slice.18 = bf16[2,256,1024]{1,2,0:T(8,128)(2,1)S(1)} dynamic-update-slice(bf16[2,256,1024]{1,2,0:T(8,128)(2,1)S(1)} %dynamic_update_slice.17, bf16[2,64,1024]{1,2,0:T(8,128)(2,1)S(1)} %bitcast.114, s32[]{:T(128)} %constant.42.clone.1, s32[]{:T(128)S(6)} %select_n.60, s32[]{:T(128)} %constant.42.clone.1) | dynamic-update-slice | bytes 524292 | tf_op jit(solution)/shard_map/dynamic_update_slice | solution.py:29
  49.4 0.0 collective-permute-done.3
  49.5 1.4 %copy.96 = bf16[2,64,1,1024]{1,3,0,2:T(8,128)(2,1)S(1)} copy(bf16[2,64,1,1024]{3,2,1,0:T(2,128)(2,1)} %collective-permute-done.3) | data formatting | bytes 524288 | tf_op jit(solution)/shard_map/squeeze | solution.py:86
  50.9 3.7 %dynamic_update_slice.19 = bf16[2,256,1024]{1,2,0:T(8,128)(2,1)S(1)} dynamic-update-slice(bf16[2,256,1024]{1,2,0:T(8,128)(2,1)S(1)} %dynamic_update_slice.18, bf16[2,64,1024]{1,2,0:T(8,128)(2,1)S(1)} %bitcast.112, s32[]{:T(128)} %constant.42.clone.1, s32[]{:T(128)S(6)} %select_n.62, s32[]{:T(128)} %constant.42.clone.1) | dynamic-update-slice | bytes 524292 | tf_op jit(solution)/shard_map/dynamic_update_slice | solution.py:29
  54.6 0.1 fusion.35
  54.7 0.0 all-to-all-done
  54.8 0.1 copy.75
  54.9 0.1 copy.76
  55.0 2.0 %fusion.39 = (f32[2,4,256]{2,1,0:T(4,128)S(1)}, bf16[2,4,256,256]{2,3,1,0:T(8,128)(2,1)}) fusion(pred[256,256]{0,1:T(8,128)(4,1)S(1)} %fusion.24, bf16[256,2,128,1]{0,2,3,1:T(8,128)(2,1)S(1)} %bitcast.122, bf16[256,2,4,128]{0,3,2,1:T(8,128)(2,1)S(1)} %bitcast.118), kind=kOutput, calls=%fused_computation.65 | convolution fusion | flops 272105728 | bytes 1777664 | tf_op jit(solution)/shard_map/sub | solution.py:109
  57.0 1.5 %fusion.15 = bf16[256,2,4,128]{0,3,2,1:T(8,128)(2,1)S(1)} fusion(bf16[256,2,128,1]{0,2,3,1:T(8,128)(2,1)S(1)} %bitcast.120, bf16[2,4,256,256]{2,3,1,0:T(8,128)(2,1)} %get-tuple-element.26, f32[256]{0:T(256)S(1)} %compare_convert_fusion, f32[256,2,4]{0,2,1:T(4,128)S(1)} %bitcast.127), kind=kOutput, calls=%fused_computation.21 | convolution fusion | flops 135004160 | bytes 1713152 | tf_op jit(solution)/shard_map/kgqs,skd->qkgd/dot_general | solution.py:112
  58.5 0.3 copy.80
  58.9 0.4 convert_element_type.67
  59.2 0.1 copy.65
  59.3 0.1 copy.66
  59.4 2.0 %fusion.40 = (f32[2,4,256]{2,1,0:T(4,128)S(1)}, bf16[2,4,256,256]{2,3,1,0:T(8,128)(2,1)}) fusion(pred[256,256]{0,1:T(8,128)(4,1)S(1)} %fusion.25, bf16[256,2,128,1]{0,2,3,1:T(8,128)(2,1)S(1)} %bitcast.121, bf16[256,2,4,128]{0,3,2,1:T(8,128)(2,1)S(1)} %bitcast.117), kind=kOutput, calls=%fused_computation.66 | convolution fusion | flops 272105728 | bytes 1777664 | tf_op jit(solution)/shard_map/sub | solution.py:109
  61.4 1.5 %fusion.14 = bf16[256,2,4,128]{0,3,2,1:T(8,128)(2,1)S(1)} fusion(bf16[256,2,128,1]{0,2,3,1:T(8,128)(2,1)S(1)} %bitcast.119, bf16[2,4,256,256]{2,3,1,0:T(8,128)(2,1)} %get-tuple-element.28, f32[256]{0:T(256)S(1)} %compare_convert_fusion.1, f32[256,2,4]{0,2,1:T(4,128)S(1)} %bitcast.128), kind=kOutput, calls=%fused_computation.20 | convolution fusion | flops 135004160 | bytes 1713152 | tf_op jit(solution)/shard_map/kgqs,skd->qkgd/dot_general | solution.py:112
  63.0 0.3 copy.74
  63.3 0.4 convert_element_type.63
  63.7 0.1 pad_maximum_fusion.1
  63.8 0.1 copy.81
  63.9 16.2 %all_to_all.36 = bf16[2,4,64,1024]{3,2,0,1:T(8,128)(2,1)S(1)} all-to-all(bf16[2,4,64,1024]{3,2,0,1:T(8,128)(2,1)S(1)} %copy.81), channel_id=1, replica_groups=mesh['section'=4,'dp'=2,'seq'=4] {'seq'}, dimensions={1} | all-to-all | bytes 2097152 | tf_op jit(solution)/shard_map/all_to_all | solution.py:140
  80.1 0.1 copy.99
  80.2 1.6 %collective-permute-start.4 = (bf16[2,1,64,4096]{3,2,0,1:T(8,128)(2,1)S(1)}, bf16[2,1,64,4096]{3,2,0,1:T(8,128)(2,1)S(1)}, u32[]{:S(2)}, u32[]{:S(2)}) collective-permute-start(bf16[2,1,64,4096]{3,2,0,1:T(8,128)(2,1)S(1)} %bitcast.115), channel_id=1, source_target_pairs={{0,8},{8,16},{16,24},{24,0},{1,9},{9,17},{17,25},{25,1},{2,10},{10... | collective-permute-start | bytes 3145736 | tf_op jit(solution)/shard_map/ppermute | solution.py:52
  81.7 22.3 %collective-permute-done.4 = bf16[2,1,64,4096]{3,2,0,1:T(8,128)(2,1)S(1)} collective-permute-done((bf16[2,1,64,4096]{3,2,0,1:T(8,128)(2,1)S(1)}, bf16[2,1,64,4096]{3,2,0,1:T(8,128)(2,1)S(1)}, u32[]{:S(2)}, u32[]{:S(2)}) %collective-permute-start.4) | collective-permute-done | bytes 1048608 | tf_op jit(solution)/shard_map/ppermute | solution.py:52
  104.0 1.0 copy.105
  (4 shorter events, 0.1 us)
Async XLA Ops:
  4.9 2.1 %copy-start = (s32[1,4,8]{2,1,0:T(4,128)S(1)}, s32[1,4,8]{2,1,0:T(4,128)}, u32[]{:S(2)}) copy-start(s32[1,4,8]{2,1,0:T(4,128)} %param.6) | copy-start | bytes 388
  4.9 3.9 %copy-start.1 = (s32[1,4]{1,0:T(1,128)S(1)}, s32[1,4]{1,0:T(1,128)}, u32[]{:S(2)}) copy-start(s32[1,4]{1,0:T(1,128)} %param.5) | copy-start | bytes 52
  6.4 3.4 %collective-permute-start = (bf16[1,64,6144]{2,1,0:T(8,128)(2,1)S(1)}, bf16[1,64,6144]{2,1,0:T(8,128)(2,1)S(1)}, u32[]{:S(2)}, u32[]{:S(2)}) collective-permute-start(bf16[1,64,6144]{2,1,0:T(8,128)(2,1)S(1)} %get-tuple-element.8), channel_id=1, source_target_pairs={{0,4},{4,0},{1,5},{5,1},{2,6},{6,2},{3,7},{7,3},{8,12},{12,8},{9,1... | collective-permute-start | bytes 2359304 | tf_op jit(solution)/shard_map/ppermute | solution.py:46
  14.3 15.6 %collective-permute-start.1 = (bf16[2,64,1,1024]{3,2,1,0:T(2,128)(2,1)}, bf16[2,64,1,1024]{3,2,1,0:T(2,128)(2,1)}, u32[]{:S(2)}, u32[]{:S(2)}) collective-permute-start(bf16[2,64,1,1024]{3,2,1,0:T(2,128)(2,1)} %get-tuple-element.13), channel_id=1, source_target_pairs={{0,1},{1,0},{2,3},{3,2},{4,5},{5,4},{6,7},{7,6},{8,9},{9,8},{10,11... | collective-permute-start | bytes 786440 | tf_op jit(solution)/shard_map/ppermute | solution.py:26
  16.8 29.2 %collective-permute-start.2 = (bf16[2,64,1,1024]{3,2,1,0:T(2,128)(2,1)}, bf16[2,64,1,1024]{3,2,1,0:T(2,128)(2,1)}, u32[]{:S(2)}, u32[]{:S(2)}) collective-permute-start(bf16[2,64,1,1024]{3,2,1,0:T(2,128)(2,1)} %get-tuple-element.12), channel_id=1, source_target_pairs={{0,2},{1,3},{2,0},{3,1},{4,6},{5,7},{6,4},{7,5},{8,10},{9,11},{10,... | collective-permute-start | bytes 786440 | tf_op jit(solution)/shard_map/ppermute | solution.py:26
  18.3 31.1 %collective-permute-start.3 = (bf16[2,64,1,1024]{3,2,1,0:T(2,128)(2,1)}, bf16[2,64,1,1024]{3,2,1,0:T(2,128)(2,1)}, u32[]{:S(2)}, u32[]{:S(2)}) collective-permute-start(bf16[2,64,1,1024]{3,2,1,0:T(2,128)(2,1)} %get-tuple-element.11), channel_id=1, source_target_pairs={{0,3},{1,2},{2,1},{3,0},{4,7},{5,6},{6,5},{7,4},{8,11},{9,10},{10,... | collective-permute-start | bytes 786440 | tf_op jit(solution)/shard_map/ppermute | solution.py:26
  19.4 35.3 %all-to-all-start = ((bf16[2,64,4,512]{3,1,0,2:T(8,128)(2,1)}), bf16[2,64,4,512]{3,1,0,2:T(8,128)(2,1)S(1)}, u32[]{:S(2)}, u32[]{:S(2)}) async-start(bf16[2,64,4,512]{3,1,0,2:T(8,128)(2,1)} %copy.63), calls=%async_computation | async-start | bytes 1048576 | tf_op jit(solution)/shard_map/all_to_all | solution.py:76
  80.2 23.8 %collective-permute-start.4 = (bf16[2,1,64,4096]{3,2,0,1:T(8,128)(2,1)S(1)}, bf16[2,1,64,4096]{3,2,0,1:T(8,128)(2,1)S(1)}, u32[]{:S(2)}, u32[]{:S(2)}) collective-permute-start(bf16[2,1,64,4096]{3,2,0,1:T(8,128)(2,1)S(1)} %bitcast.115), channel_id=1, source_target_pairs={{0,8},{8,16},{16,24},{24,0},{1,9},{9,17},{17,25},{25,1},{2,10},{10... | collective-permute-start | bytes 3145736 | tf_op jit(solution)/shard_map/ppermute | solution.py:52
